TPU v7x, 32 devices: a whole 2x2x4 slice. The times are simulated.
32 devices in a mesh: seq: 8 (over z, y), fsdp: 4 (over x, core).
Axes of the slice: x: 2, y: 2, z: 4, core: 2. Of those that a mesh axis runs over, the one named last changes fastest.
Arguments:
- tokens: bfloat16 [2048, 2048], P('seq', 'fsdp'), may hold values from -6 to 6
- deal_order: int32 [8, 8], replicated, may hold values from 0 to 7, each once within a row
- lengths: int32 [4], replicated, may hold values from 1 to 1024, 2048 in all
- x_weight: bfloat16 [2048, 1536], P(None, 'fsdp'), may hold values from -0.0390625 to 0.0390625
- z_weight: bfloat16 [2048, 1536], P(None, 'fsdp'), may hold values from -0.125 to 0.125
- shared_weight: bfloat16 [2048, 512], P('fsdp'), may hold values from -0.0390625 to 0.0390625
- step_weight: bfloat16 [2048, 24], P(None, 'fsdp'), may hold values from -0.125 to 0.125
- conv_heads: float32 [4, 1536], P(None, 'fsdp'), may hold values from -3 to 3
- conv_shared: float32 [4, 512], replicated, may hold values from -3 to 3
- step_bias: float32 [24], P('fsdp'), as said below
- decay_log: float32 [24], P('fsdp'), may hold values from -7.1 to -2.8, as said below
- skip_gain: float32 [24], P('fsdp'), may hold values from 0.5 to 1.5
Outputs:
- mixed: bfloat16 [2048, 1536], P('seq', 'fsdp')
Inputs may be any that keep to these rules, and one draw needn't show every extreme that they name: `deal_order`: each row is a permutation of 0 to 7. The lengths sum to 2048. `decay_log`: one value a head. `step_bias`: one value a head.
All inputs are finite; a program needn't handle non-finite values.
Results may differ from a plain program's by a relative error of at most 0.0095.
Values may be sent and summed in bfloat16 or wider, within the bound.
No kernel may reach another device: no remote copies, remote signals or barrier semaphores. Data moves between devices by JAX's collectives and lax.ppermute only.
A program may use at most 128 MiB of HBM per device.

v0:
```python
import jax
import jax.numpy as jnp
from jax import lax
from jax.sharding import PartitionSpec as P

precise = lax.Precision.HIGHEST


def shifted(array, axis, by):
    count = lax.axis_size(axis)
    pairs = [(i, i + by) for i in range(count) if 0 <= i + by < count]
    return lax.ppermute(array, axis, pairs)


def combine_packed(earlier, later):
    rows = later.shape[1] - 1
    d_e, d_l = (earlier[:, rows:, :], later[:, rows:, :])
    return jnp.concatenate([d_l * earlier[:, :rows, :] + later[:, :rows, :], d_e * d_l], axis=1)


def received(packed, axis, by):
    place = lax.axis_index(axis)
    got = shifted(packed, axis, by)
    rows = packed.shape[1] - 1
    missing = (place < by).astype(packed.dtype)
    return got.at[:, rows:, :].add(missing)


def exclusive_scan(packed, axis):
    count = lax.axis_size(axis)
    if count == 1:
        return received(packed, axis, 1)
    held = received(packed, axis, 1)
    if count > 2:
        held = combine_packed(received(packed, axis, 2), held)
    cover = 2
    while cover < count - 1:
        held = combine_packed(received(held, axis, cover), held)
        cover *= 2
    return held


def segment_of(positions, lengths):
    prompt_ends = jnp.cumsum(lengths)
    counted = (positions[:, None] >= prompt_ends[None, :]).astype(jnp.int32)
    return jnp.sum(counted, axis=1)


def causal_conv(extended, segment_ids, weights, conv_width):
    out_rows = extended.shape[0] - conv_width + 1
    target = segment_ids[conv_width - 1 :]
    running = jnp.zeros((out_rows, extended.shape[1]), jnp.float32)
    for tap_index in range(conv_width):
        matched = (segment_ids[tap_index : tap_index + out_rows] == target).astype(jnp.float32)
        running = (
            running
            + weights[tap_index][None, :]
            * extended[tap_index : tap_index + out_rows]
            * matched[:, None]
        )
    return running


def local_terms(x_heads, b_rows, c_rows, step_size, decay_log, segment_ids, seg_before):
    log_decay = -jnp.exp(decay_log)[None, :] * step_size
    cum_decay = jnp.cumsum(log_decay, axis=0)
    positions_in = jnp.arange(x_heads.shape[0], dtype=jnp.int32)
    same_prompt = (segment_ids[:, None] == segment_ids[None, :]) & (
        positions_in[:, None] >= positions_in[None, :]
    )
    decay_gap = cum_decay.T[:, :, None] - cum_decay.T[:, None, :]
    decay_matrix = jnp.exp(jnp.where(same_prompt[None], decay_gap, -jnp.inf))
    scores = jnp.dot(c_rows, b_rows.T, precision=precise)
    x_step = x_heads * step_size[:, :, None]
    intra = jnp.einsum("hts,shp->thp", scores[None] * decay_matrix, x_step, precision=precise)
    to_end = jnp.exp(
        jnp.where(
            (segment_ids == segment_ids[-1])[:, None], cum_decay[-1][None, :] - cum_decay, -jnp.inf
        )
    )
    state_out = jnp.einsum("shp,sn->hpn", x_step * to_end[:, :, None], b_rows, precision=precise)
    carried = segment_ids == seg_before
    carry_in = jnp.exp(jnp.where(carried[:, None], cum_decay, -jnp.inf))
    block_decay = jnp.where(carried[-1], jnp.exp(cum_decay[-1]), 0.0)
    return (intra, state_out, carry_in, block_decay)


def per_device(
    tokens,
    deal_order,
    lengths,
    x_weight,
    z_weight,
    shared_weight,
    step_weight,
    conv_heads,
    conv_shared,
    step_bias,
    decay_log,
    skip_gain,
):
    seq_count = lax.axis_size("seq")
    own_index = lax.axis_index("seq")
    tok_dev = tokens.shape[0]
    piece_rows = tok_dev // seq_count
    slot_rows = tokens.reshape(seq_count, piece_rows, tokens.shape[1])
    arrived = lax.all_to_all(slot_rows, "seq", split_axis=0, concat_axis=0, tiled=True)
    dealt_row = lax.dynamic_slice_in_dim(deal_order, own_index, 1, 0)[0]
    inverse = jnp.argsort(dealt_row)
    stream_block = jnp.take(arrived, inverse, axis=0).reshape(tok_dev, tokens.shape[1])
    inner_dev = x_weight.shape[1]
    heads_dev = step_weight.shape[1]
    head_dim = inner_dev // heads_dev
    state_dim = shared_weight.shape[1] // 2
    w_full = lax.all_gather(shared_weight, "fsdp", axis=0, tiled=True)
    weight_list = (x_weight, z_weight, step_weight, w_full)
    feature_part = lax.all_gather(stream_block, "fsdp", axis=1, tiled=True)
    x_acc, z_acc, step_acc, bc_acc = tuple(
        (
            jnp.dot(feature_part, weight, preferred_element_type=jnp.float32)
            for weight in weight_list
        )
    )
    x_raw = x_acc.astype(jnp.bfloat16)
    z_raw = z_acc.astype(jnp.bfloat16)
    bc_raw = bc_acc.astype(jnp.bfloat16)
    step_size = jax.nn.softplus(step_acc + step_bias[None, :])
    mixed_in = jnp.concatenate([x_raw, bc_raw], axis=1)
    conv_width = conv_heads.shape[0]
    prior_rows = shifted(mixed_in[tok_dev - conv_width + 1 :], "seq", 1)
    first_pos = own_index * tok_dev
    positions = first_pos - (conv_width - 1) + jnp.arange(tok_dev + conv_width - 1, dtype=jnp.int32)
    seg_ext = segment_of(positions, lengths)
    extended = jnp.concatenate([prior_rows, mixed_in], axis=0).astype(jnp.float32)
    activated = jax.nn.silu(
        causal_conv(
            extended, seg_ext, jnp.concatenate([conv_heads, conv_shared], axis=1), conv_width
        )
    )
    segment_ids = seg_ext[conv_width - 1 :]
    seg_before = jnp.where(own_index == 0, -1, seg_ext[conv_width - 2])
    x_heads = activated[:, :inner_dev].reshape(tok_dev, heads_dev, head_dim)
    b_rows = activated[:, inner_dev : inner_dev + state_dim]
    c_rows = activated[:, inner_dev + state_dim :]
    intra, state_out, carry_in, block_decay = local_terms(
        x_heads, b_rows, c_rows, step_size, decay_log, segment_ids, seg_before
    )
    packed = jnp.concatenate(
        [state_out, jnp.broadcast_to(block_decay[:, None, None], (heads_dev, 1, state_dim))], axis=1
    )
    state_in = exclusive_scan(packed, "seq")[:, :head_dim, :]
    incoming = jnp.einsum("tn,hpn->thp", c_rows, state_in, precision=precise)
    y_block = intra + carry_in[:, :, None] * incoming + skip_gain[None, :, None] * x_heads
    gated = (y_block.reshape(tok_dev, inner_dev) * jax.nn.silu(z_raw.astype(jnp.float32))).astype(
        jnp.bfloat16
    )
    ordered = gated.reshape(seq_count, piece_rows, inner_dev)
    outgoing = jnp.take(ordered, dealt_row, axis=0)
    returned = lax.all_to_all(outgoing, "seq", split_axis=0, concat_axis=0, tiled=True)
    return returned.reshape(tok_dev, inner_dev)


def solution(mesh):
    return jax.shard_map(
        per_device,
        mesh=mesh,
        in_specs=(
            P("seq", "fsdp"),
            P(),
            P(),
            P(None, "fsdp"),
            P(None, "fsdp"),
            P("fsdp", None),
            P(None, "fsdp"),
            P(None, "fsdp"),
            P(),
            P("fsdp"),
            P("fsdp"),
            P("fsdp"),
        ),
        out_specs=P("seq", "fsdp"),
        check_vma=False,
    )
```

profile of v0, /device:TPU:0, one launch (start us, length us, event | category | flops | bytes accessed | tf_op | source)
XLA Modules:
  0.0 161.2 jit_solution(1924981026122222076)
XLA Ops:
  6.6 7.4 %all-to-all-start = ((bf16[8,32,512]{2,1,0:T(8,128)(2,1)}), bf16[8,32,512]{2,1,0:T(8,128)(2,1)S(1)}, u32[]{:S(2)}, u32[]{:S(2)}) async-start(bf16[8,32,512]{2,1,0:T(8,128)(2,1)} %bitcast.85), calls=%async_computation | async-start | bytes 524288 | tf_op jit(solution)/shard_map/all_to_all | solution.py:107
  14.0 1.3 compare_and_fusion.1
  15.3 1.0 sort.17
  16.5 6.4 %all-to-all-done = bf16[8,32,512]{2,1,0:T(8,128)(2,1)S(1)} async-done(((bf16[8,32,512]{2,1,0:T(8,128)(2,1)}), bf16[8,32,512]{2,1,0:T(8,128)(2,1)S(1)}, u32[]{:S(2)}, u32[]{:S(2)}) %all-to-all-start) | async-done | bytes 262176 | tf_op jit(solution)/shard_map/all_to_all | solution.py:107
  22.9 0.6 gather_fusion
  23.5 0.8 bitcast_select_fusion
  24.4 0.7 all-gather.5.cloned.1.call-update
  25.4 0.6 fusion.53
  26.5 1.3 broadcast_compare_fusion
  27.9 0.7 slice.199
  28.5 0.6 slice_reduce_fusion.4
  29.2 11.1 %all-gather.3.cloned.1.call-done = bf16[256,2048]{1,0:T(8,128)(2,1)} async-done(((bf16[256,512]{1,0:T(8,128)(2,1)}), bf16[256,2048]{1,0:T(8,128)(2,1)}) %all-gather.3.cloned.1.call-update) | async-done | bytes 1048592 | tf_op jit(solution)/shard_map/all_gather | solution.py:117
  40.2 1.6 %fusion.41 = (f32[6,256]{1,0:T(8,128)S(1)}, f32[256,6]{0,1:T(8,128)S(1)}) fusion(f32[6]{0:T(128)S(1)} %exponential_negate_fusion, f32[6]{0:T(128)S(1)} %copy-done.19, bf16[256,2048]{1,0:T(8,128)(2,1)} %all-gather.3.cloned.1.call-done, bf16[2048,6]{0,1:T(8,128)(2,1)S(1)} %copy-done.4), kind=kOutput, calls=%fused_computation.64 | convolution fusion | flops 6303744 | bytes 1085488 | tf_op jit(solution)/shard_map/dot_general | solution.py:120
  41.9 1.8 %reduce-window.19 = f32[6,2,128]{2,1,0:T(2,128)S(1)} reduce-window(f32[6,2,128]{2,1,0:T(2,128)S(1)} %reshape.288, f32[]{:T(128)} %constant.149.clone.1), window={size=1x1x128 pad=0_0x0_0x127_0}, to_apply=%region_3.4 | reduce-window | flops 195072 | bytes 12292 | tf_op jit(solution)/shard_map/reduce-window.1
  44.3 0.4 copy-done.7
  44.7 0.7 select_exponential_fusion.1
  45.4 1.9 %convolution_convert_fusion.2 = bf16[256,384]{1,0:T(8,128)(2,1)S(1)} fusion(bf16[256,2048]{1,0:T(8,128)(2,1)} %all-gather.3.cloned.1.call-done, bf16[2048,384]{1,0:T(8,128)(2,1)S(1)} %copy-done), kind=kOutput, calls=%fused_computation.14 | convolution fusion | flops 402751488 | bytes 2818048 | tf_op jit(solution)/shard_map/dot_general | solution.py:120
  47.3 17.1 %all-gather.5.cloned.1.call-done = bf16[2048,512]{1,0:T(8,128)(2,1)} async-done(((bf16[512,512]{1,0:T(8,128)(2,1)}), bf16[2048,512]{1,0:T(8,128)(2,1)}) %all-gather.5.cloned.1.call-update) | async-done | bytes 2097168 | tf_op jit(solution)/shard_map/all_gather | solution.py:115
  64.4 2.3 %convolution_convert_fusion = bf16[256,512]{1,0:T(8,128)(2,1)S(1)} fusion(bf16[256,2048]{1,0:T(8,128)(2,1)S(1)} %copy-done.1, bf16[2048,512]{1,0:T(8,128)(2,1)} %all-gather.5.cloned.1.call-done), kind=kOutput, calls=%fused_computation.8 | convolution fusion | flops 537001984 | bytes 3407872 | tf_op jit(solution)/shard_map/dot_general | solution.py:120
  66.8 3.4 %collective-permute-start = (bf16[3,896]{1,0:T(4,128)(2,1)S(1)}, bf16[3,896]{1,0:T(4,128)(2,1)S(1)}, u32[]{:S(2)}, u32[]{:S(2)}) collective-permute-start(bf16[3,896]{1,0:T(4,128)(2,1)S(1)} %pad_maximum_fusion.3), channel_id=1, source_target_pairs={{0,4},{4,8},{8,12},{12,16},{16,20},{20,24},{24,28},{1,5},{5,9},{9,... | collective-permute-start | bytes 16136 | tf_op jit(solution)/shard_map/ppermute | solution.py:12
  70.2 1.2 broadcast_select_fusion.1
  71.7 0.7 divide_multiply_fusion
  72.4 0.8 slice.219
  73.1 1.9 %copy.39 = f32[256,384]{0,1:T(8,128)} copy(f32[256,384]{1,0:T(8,128)} %slice.219) | data formatting | bytes 786432 | tf_op jit(solution)/shard_map/slice | solution.py:142
  75.1 1.5 fusion.25
  76.5 0.7 broadcast_in_dim.104
  77.3 0.8 pad_maximum_fusion
  78.1 5.9 %collective-permute-start.2 = (f32[6,65,256]{2,1,0:T(8,128)}, f32[6,65,256]{2,1,0:T(8,128)}, u32[]{:S(2)}, u32[]{:S(2)}) collective-permute-start(f32[6,65,256]{2,1,0:T(8,128)} %pad_maximum_fusion), channel_id=1, source_target_pairs={{0,8},{4,12},{8,16},{12,20},{16,24},{20,28},{1,9},{5,13},{9,17},{1... | collective-permute-start | bytes 1198088 | tf_op jit(solution)/shard_map/ppermute | solution.py:12
  83.9 3.2 %collective-permute-start.1 = (f32[6,65,256]{2,1,0:T(8,128)}, f32[6,65,256]{2,1,0:T(8,128)}, u32[]{:S(2)}, u32[]{:S(2)}) collective-permute-start(f32[6,65,256]{2,1,0:T(8,128)} %pad_maximum_fusion), channel_id=1, source_target_pairs={{0,4},{4,8},{8,12},{12,16},{16,20},{20,24},{24,28},{1,5},{5,9},{9,... | collective-permute-start | bytes 1198088 | tf_op jit(solution)/shard_map/ppermute | solution.py:12
  87.2 0.7 slice.182
  87.8 0.8 fusion.49
  88.7 0.9 fusion.31
  89.5 2.6 %collective-permute-done.2 = f32[6,65,256]{2,1,0:T(8,128)} collective-permute-done((f32[6,65,256]{2,1,0:T(8,128)}, f32[6,65,256]{2,1,0:T(8,128)}, u32[]{:S(2)}, u32[]{:S(2)}) %collective-permute-start.2) | collective-permute-done | bytes 399392 | tf_op jit(solution)/shard_map/ppermute | solution.py:12
  92.1 3.0 %collective-permute-done.1 = f32[6,65,256]{2,1,0:T(8,128)} collective-permute-done((f32[6,65,256]{2,1,0:T(8,128)}, f32[6,65,256]{2,1,0:T(8,128)}, u32[]{:S(2)}, u32[]{:S(2)}) %collective-permute-start.1) | collective-permute-done | bytes 399392 | tf_op jit(solution)/shard_map/ppermute | solution.py:12
  95.1 0.8 fusion.47
  96.0 1.2 slice_add_fusion
  97.2 10.9 %collective-permute-start.3 = (f32[6,65,256]{2,1,0:T(8,128)S(1)}, f32[6,65,256]{2,1,0:T(8,128)S(1)}, u32[]{:S(2)}, u32[]{:S(2)}) collective-permute-start(f32[6,65,256]{2,1,0:T(8,128)S(1)} %pad_maximum_fusion.1), channel_id=1, source_target_pairs={{0,8},{4,12},{8,16},{12,20},{16,24},{20,28},{1,9},{5,13},{9,17},{1... | collective-permute-start | bytes 1198088 | tf_op jit(solution)/shard_map/ppermute | solution.py:12
  108.1 0.6 pad_clamp_fusion
  108.7 1.4 fusion.10
  110.2 5.7 %collective-permute-done.3 = f32[6,65,256]{2,1,0:T(8,128)S(1)} collective-permute-done((f32[6,65,256]{2,1,0:T(8,128)S(1)}, f32[6,65,256]{2,1,0:T(8,128)S(1)}, u32[]{:S(2)}, u32[]{:S(2)}) %collective-permute-start.3) | collective-permute-done | bytes 399392 | tf_op jit(solution)/shard_map/ppermute | solution.py:12
  116.0 5.3 %collective-permute-start.4 = (f32[6,65,256]{2,1,0:T(8,128)S(1)}, f32[6,65,256]{2,1,0:T(8,128)S(1)}, u32[]{:S(2)}, u32[]{:S(2)}) collective-permute-start(f32[6,65,256]{2,1,0:T(8,128)S(1)} %pad_maximum_fusion.2), channel_id=1, source_target_pairs={{0,16},{4,20},{8,24},{12,28},{1,17},{5,21},{9,25},{13,29},{2,18},{... | collective-permute-start | bytes 1198088 | tf_op jit(solution)/shard_map/ppermute | solution.py:12
  121.7 1.9 %fusion.5 = f32[256,6,64]{0,2,1:T(8,128)S(1)} fusion(f32[6,256]{1,0:T(8,128)S(1)} %bitcast.90, f32[256,256]{1,0:T(8,128)S(1)} %fusion.33, pred[256,256]{1,0:T(8,128)(4,1)S(1)} %fusion.31, f32[256,6,64]{0,2,1:T(8,128)S(1)} %bitcast.80, f32[256,6]{0,1:T(8,128)S(1)} %get-tuple-element.76), kind=kOutput, calls=%fused_computation.7 | convolution fusion | flops 303267840 | bytes 1126400 | tf_op jit(solution)/shard_map/hts,shp->thp/dot_general | solution.py:75
  123.6 4.5 %collective-permute-done.4 = f32[6,65,256]{2,1,0:T(8,128)S(1)} collective-permute-done((f32[6,65,256]{2,1,0:T(8,128)S(1)}, f32[6,65,256]{2,1,0:T(8,128)S(1)}, u32[]{:S(2)}, u32[]{:S(2)}) %collective-permute-start.4) | collective-permute-done | bytes 399392 | tf_op jit(solution)/shard_map/ppermute | solution.py:12
  128.1 0.5 fusion.9
  128.8 1.1 multiply_convert_fusion
  129.9 0.7 gather_fusion.1
  130.8 22.9 %all_to_all.10 = bf16[8,32,384]{2,1,0:T(8,128)(2,1)S(1)} all-to-all(bf16[8,32,384]{2,1,0:T(8,128)(2,1)S(1)} %broadcast_select_fusion), channel_id=1, replica_groups=mesh['seq'=8,'fsdp'=4] {'seq'}, dimensions={0} | all-to-all | bytes 393216 | tf_op jit(solution)/shard_map/all_to_all | solution.py:159
  153.7 0.7 copy.63
  (82 shorter events, 2.3 us)
Async XLA Ops:
  6.5 38.8 %copy-start = (bf16[2048,384]{1,0:T(8,128)(2,1)S(1)}, bf16[2048,384]{1,0:T(8,128)(2,1)}, u32[]{:S(2)}) copy-start(bf16[2048,384]{1,0:T(8,128)(2,1)} %param.23) | copy-start | bytes 4718596
  6.5 18.5 %copy-start.21 = (s32[4]{0:T(128)S(1)}, s32[4]{0:T(128)}, u32[]{:S(2)}) copy-start(s32[4]{0:T(128)} %param.22) | copy-start | bytes 52
  6.5 22.0 %copy-start.14 = (f32[4,384]{1,0:T(4,128)S(1)}, f32[4,384]{1,0:T(4,128)}, u32[]{:S(2)}) copy-start(f32[4,384]{1,0:T(4,128)} %param.27) | copy-start | bytes 18436
  6.5 22.0 %copy-start.13 = (f32[4,512]{1,0:T(4,128)S(1)}, f32[4,512]{1,0:T(4,128)}, u32[]{:S(2)}) copy-start(f32[4,512]{1,0:T(4,128)} %param.28) | copy-start | bytes 24580
  6.5 22.6 %copy-start.22 = (f32[6]{0:T(128)S(1)}, f32[6]{0:T(128)}, u32[]{:S(2)}) copy-start(f32[6]{0:T(128)} %param.30) | copy-start | bytes 76
  6.5 33.7 %copy-start.19 = (f32[6]{0:T(128)S(1)}, f32[6]{0:T(128)}, u32[]{:S(2)}) copy-start(f32[6]{0:T(128)} %param.29) | copy-start | bytes 76
  6.6 33.7 %copy-start.4 = (bf16[2048,6]{0,1:T(8,128)(2,1)S(1)}, bf16[2048,6]{0,1:T(8,128)(2,1)}, u32[]{:S(2)}) copy-start(bf16[2048,6]{0,1:T(8,128)(2,1)} %param.26) | copy-start | bytes 73732
  6.6 16.3 %all-to-all-start = ((bf16[8,32,512]{2,1,0:T(8,128)(2,1)}), bf16[8,32,512]{2,1,0:T(8,128)(2,1)S(1)}, u32[]{:S(2)}, u32[]{:S(2)}) async-start(bf16[8,32,512]{2,1,0:T(8,128)(2,1)} %bitcast.85), calls=%async_computation | async-start | bytes 524288 | tf_op jit(solution)/shard_map/all_to_all | solution.py:107
  14.0 26.2 %all-gather.3.cloned.1.call-start = ((), (), s32[]{:S(2)}) async-start(), calls=%async_computation.2 | async-start | bytes 1310720 | tf_op jit(solution)/shard_map/all_gather | solution.py:117
  24.3 40.1 %all-gather.5.cloned.1.call-start = ((), (), s32[]{:S(2)}) async-start(), calls=%async_computation.3 | async-start | bytes 2621440 | tf_op jit(solution)/shard_map/all_gather | solution.py:115
  25.4 14.9 %copy-start.5 = (s32[259]{0:T(512)}, s32[259]{0:T(512)S(1)}, u32[]{:S(2)}) copy-start(s32[259]{0:T(512)S(1)} %convert_reduce_fusion) | copy-start | bytes 3112
  41.9 22.5 %copy-start.1 = (bf16[256,2048]{1,0:T(8,128)(2,1)S(1)}, bf16[256,2048]{1,0:T(8,128)(2,1)}, u32[]{:S(2)}) copy-start(bf16[256,2048]{1,0:T(8,128)(2,1)} %all-gather.3.cloned.1.call-done) | copy-start | bytes 3145732
  44.1 0.6 copy-start.7
  66.7 4.9 %copy-start.9 = (f32[896]{0:T(1024)S(1)}, f32[896]{0:T(1024)}, u32[]{:S(2)}) copy-start(f32[896]{0:T(1024)} %get-tuple-element.55) | copy-start | bytes 10756
  66.7 4.9 %copy-start.10 = (f32[896]{0:T(1024)S(1)}, f32[896]{0:T(1024)}, u32[]{:S(2)}) copy-start(f32[896]{0:T(1024)} %get-tuple-element.56) | copy-start | bytes 10756
  66.7 4.9 %copy-start.11 = (f32[896]{0:T(1024)S(1)}, f32[896]{0:T(1024)}, u32[]{:S(2)}) copy-start(f32[896]{0:T(1024)} %get-tuple-element.57) | copy-start | bytes 10756
  66.7 4.9 %copy-start.12 = (f32[896]{0:T(1024)S(1)}, f32[896]{0:T(1024)}, u32[]{:S(2)}) copy-start(f32[896]{0:T(1024)} %get-tuple-element.58) | copy-start | bytes 10756
  66.7 4.9 %copy-start.15 = (f32[256]{0:T(256)S(1)}, f32[256]{0:T(256)}, u32[]{:S(2)}) copy-start(f32[256]{0:T(256)} %get-tuple-element.69) | copy-start | bytes 3076
  66.8 4.9 %copy-start.16 = (f32[256]{0:T(256)S(1)}, f32[256]{0:T(256)}, u32[]{:S(2)}) copy-start(f32[256]{0:T(256)} %get-tuple-element.70) | copy-start | bytes 3076
  66.8 4.9 %copy-start.17 = (f32[256]{0:T(256)S(1)}, f32[256]{0:T(256)}, u32[]{:S(2)}) copy-start(f32[256]{0:T(256)} %get-tuple-element.71) | copy-start | bytes 3076
  66.8 4.7 %collective-permute-start = (bf16[3,896]{1,0:T(4,128)(2,1)S(1)}, bf16[3,896]{1,0:T(4,128)(2,1)S(1)}, u32[]{:S(2)}, u32[]{:S(2)}) collective-permute-start(bf16[3,896]{1,0:T(4,128)(2,1)S(1)} %pad_maximum_fusion.3), channel_id=1, source_target_pairs={{0,4},{4,8},{8,12},{12,16},{16,20},{20,24},{24,28},{1,5},{5,9},{9,... | collective-permute-start | bytes 16136 | tf_op jit(solution)/shard_map/ppermute | solution.py:12
  75.0 12.1 %copy-start.6 = (s32[259]{0:T(512)S(1)}, s32[259]{0:T(512)}, u32[]{:S(2)}) copy-start(s32[259]{0:T(512)} %copy-done.5) | copy-start | bytes 3112
  78.1 14.1 %collective-permute-start.2 = (f32[6,65,256]{2,1,0:T(8,128)}, f32[6,65,256]{2,1,0:T(8,128)}, u32[]{:S(2)}, u32[]{:S(2)}) collective-permute-start(f32[6,65,256]{2,1,0:T(8,128)} %pad_maximum_fusion), channel_id=1, source_target_pairs={{0,8},{4,12},{8,16},{12,20},{16,24},{20,28},{1,9},{5,13},{9,17},{1... | collective-permute-start | bytes 1198088 | tf_op jit(solution)/shard_map/ppermute | solution.py:12
  83.9 11.2 %collective-permute-start.1 = (f32[6,65,256]{2,1,0:T(8,128)}, f32[6,65,256]{2,1,0:T(8,128)}, u32[]{:S(2)}, u32[]{:S(2)}) collective-permute-start(f32[6,65,256]{2,1,0:T(8,128)} %pad_maximum_fusion), channel_id=1, source_target_pairs={{0,4},{4,8},{8,12},{12,16},{16,20},{20,24},{24,28},{1,5},{5,9},{9,... | collective-permute-start | bytes 1198088 | tf_op jit(solution)/shard_map/ppermute | solution.py:12
  87.8 20.9 %copy-start.3 = (bf16[2048,384]{1,0:T(8,128)(2,1)S(1)}, bf16[2048,384]{1,0:T(8,128)(2,1)}, u32[]{:S(2)}) copy-start(bf16[2048,384]{1,0:T(8,128)(2,1)} %param.24) | copy-start | bytes 4718596
  97.2 18.7 %collective-permute-start.3 = (f32[6,65,256]{2,1,0:T(8,128)S(1)}, f32[6,65,256]{2,1,0:T(8,128)S(1)}, u32[]{:S(2)}, u32[]{:S(2)}) collective-permute-start(f32[6,65,256]{2,1,0:T(8,128)S(1)} %pad_maximum_fusion.1), channel_id=1, source_target_pairs={{0,8},{4,12},{8,16},{12,20},{16,24},{20,28},{1,9},{5,13},{9,17},{1... | collective-permute-start | bytes 1198088 | tf_op jit(solution)/shard_map/ppermute | solution.py:12
  110.2 11.6 %copy-start.2 = (f32[256,384]{0,1:T(8,128)S(1)}, f32[256,384]{0,1:T(8,128)}, u32[]{:S(2)}) copy-start(f32[256,384]{0,1:T(8,128)} %copy.39) | copy-start | bytes 1179652
  110.2 11.6 %copy-start.8 = (f32[1,6,2,128]{3,1,2,0:T(8,128)S(1)}, f32[1,6,2,128]{3,1,2,0:T(8,128)}, u32[]{:S(2)}) copy-start(f32[1,6,2,128]{3,1,2,0:T(8,128)} %copy-done.7) | copy-start | bytes 18436
  115.9 12.2 %copy-start.20 = (f32[6]{0:T(128)S(1)}, f32[6]{0:T(128)}, u32[]{:S(2)}) copy-start(f32[6]{0:T(128)} %param.31) | copy-start | bytes 76
  116.0 12.2 %collective-permute-start.4 = (f32[6,65,256]{2,1,0:T(8,128)S(1)}, f32[6,65,256]{2,1,0:T(8,128)S(1)}, u32[]{:S(2)}, u32[]{:S(2)}) collective-permute-start(f32[6,65,256]{2,1,0:T(8,128)S(1)} %pad_maximum_fusion.2), channel_id=1, source_target_pairs={{0,16},{4,20},{8,24},{12,28},{1,17},{5,21},{9,25},{13,29},{2,18},{... | collective-permute-start | bytes 1198088 | tf_op jit(solution)/shard_map/ppermute | solution.py:12
  128.7 2.0 %copy-start.18 = (pred[8]{0:T(512)(128)(4,1)S(1)}, pred[8]{0:T(512)(128)(4,1)}, u32[]{:S(2)}) copy-start(pred[8]{0:T(512)(128)(4,1)} %get-tuple-element.59) | copy-start | bytes 28
Sparse Core Ops, SparseCore 0:
  24.4 15.7 all-gather.2
  41.8 22.5 all-gather.4
where the time goes:
time: 162 us; the launch traced here: 161 us
  waiting for transfers between devices  51.2 us (32%)
  starting transfers between devices  36.3 us (22%)
  blocking collectives  22.9 us (14%)
  other arithmetic  15.7 us (10%)
  between operations  14.4 us (9%)
  matrix products  11.6 us (7%)
  local copies, waits for them, and re-layouts  9.22 us (6%)
    ppermute x5, starting transfers between devices, shifted(): return lax.ppermute(array, axis, pairs)  28.8 us
    all_to_all x1, blocking collectives, per_device(): lax.all_to_all(outgoing, 'seq', split_axis=0, concat_axis=0, tiled=True)  22.9 us
    all_gather x1, waiting for transfers between devices, per_device(): w_full = lax.all_gather(shared_weight, 'fsdp', axis=0, tiled=True)  17.1 us
    ppermute x5, waiting for transfers between devices, shifted(): return lax.ppermute(array, axis, pairs)  15.9 us
    all_gather x1, waiting for transfers between devices, per_device(): feature_part = lax.all_gather(stream_block, 'fsdp', axis=1, tiled=True)  11.1 us
    all_to_all x1, starting transfers between devices, per_device(): lax.all_to_all(slot_rows, 'seq', split_axis=0, concat_axis=0, tiled=True)  7.42 us
    dot_general x4, matrix products, per_device(): jnp.dot(feature_part, weight, preferred_element_type=jnp.float32)  7.29 us
    all_to_all x1, waiting for transfers between devices, per_device(): lax.all_to_all(slot_rows, 'seq', split_axis=0, concat_axis=0, tiled=True)  6.42 us
  transfers between devices with their start and end apart: 8, of which 8 were waited for; matrix products, arithmetic and copies ran while one was open for 13% of the time, Pallas kernels for 0%

commit v1 on v0

--- a/solution.py
+++ b/solution.py
@@ -4,6 +4,18 @@
 from jax.sharding import PartitionSpec as P
 
 precise = lax.Precision.HIGHEST
+
+
+def gather_by_bits(array, axis, dim):
+    ways, here = (lax.axis_size(axis), lax.axis_index(axis))
+    grown, reach = (array, 1)
+    while reach < ways:
+        theirs = lax.ppermute(grown, axis, [(d, d ^ reach) for d in range(ways)])
+        mine_first = jnp.concatenate([grown, theirs], axis=dim)
+        theirs_first = jnp.concatenate([theirs, grown], axis=dim)
+        grown = jnp.where(here & reach == 0, mine_first, theirs_first)
+        reach = 2 * reach
+    return grown
 
 
 def shifted(array, axis, by):
@@ -114,7 +126,7 @@
     state_dim = shared_weight.shape[1] // 2
     w_full = lax.all_gather(shared_weight, "fsdp", axis=0, tiled=True)
     weight_list = (x_weight, z_weight, step_weight, w_full)
-    feature_part = lax.all_gather(stream_block, "fsdp", axis=1, tiled=True)
+    feature_part = gather_by_bits(stream_block, "fsdp", 1)
     x_acc, z_acc, step_acc, bc_acc = tuple(
         (
             jnp.dot(feature_part, weight, preferred_element_type=jnp.float32)

time: 162 us -> 140 us (0.86)
  waiting for transfers between devices: 51.2 us -> 39.7 us
  local copies, waits for them, and re-layouts: 9.22 us -> 4.26 us
  other arithmetic: 15.7 us -> 12.1 us
  matrix products: 11.6 us -> 8.26 us
    all_gather x1, waiting for transfers between devices: 17.1 us -> 0.02 us  [per_device(): w_full = lax.all_gather(shared_weight, 'fsdp', axis=0, tiled=True)]
    ppermute x0 -> x2, waiting for transfers between devices: none -> 15.4 us  [gather_by_bits(): theirs = lax.ppermute(grown, axis, [(d, d ^ reach) for d in range(ways)])]
    all_gather x1 -> x0, waiting for transfers between devices: 11.1 us -> none  [per_device(): feature_part = lax.all_gather(stream_block, 'fsdp', axis=1, tiled=True)]
    slice x2, local copies, waits for them, and re-layouts: 2.68 us -> 0.19 us  [per_device(): x_heads = activated[:, :inner_dev].reshape(tok_dev, heads_dev, head_dim)]
    dot_general x4, matrix products: 7.29 us -> 4.95 us  [per_device(): jnp.dot(feature_part, weight, preferred_element_type=jnp.float32)]
    ppermute x0 -> x2, starting transfers between devices: none -> 1.63 us  [gather_by_bits(): theirs = lax.ppermute(grown, axis, [(d, d ^ reach) for d in range(ways)])]
  transfers between devices with their start and end apart: 8 -> 9, of which waited for: 8 -> 7; matrix products, arithmetic and copies ran while one was open for 13% -> 10% of each run, Pallas kernels for 0% -> 0%
where the time goes in v1:
time: 140 us; the launch traced here: 139 us
  waiting for transfers between devices  39.7 us (28%)
  starting transfers between devices  37.7 us (27%)
  blocking collectives  22.9 us (16%)
  between operations  14.4 us (10%)
  other arithmetic  12.1 us (9%)
  matrix products  8.26 us (6%)
  local copies, waits for them, and re-layouts  4.26 us (3%)
    ppermute x5, starting transfers between devices, shifted(): return lax.ppermute(array, axis, pairs)  28.7 us
    all_to_all x1, blocking collectives, per_device(): lax.all_to_all(outgoing, 'seq', split_axis=0, concat_axis=0, tiled=True)  22.9 us
    ppermute x5, waiting for transfers between devices, shifted(): return lax.ppermute(array, axis, pairs)  17.5 us
    ppermute x2, waiting for transfers between devices, gather_by_bits(): theirs = lax.ppermute(grown, axis, [(d, d ^ reach) for d in range(ways)])  15.4 us
    all_to_all x1, starting transfers between devices, per_device(): lax.all_to_all(slot_rows, 'seq', split_axis=0, concat_axis=0, tiled=True)  7.29 us
    all_to_all x1, waiting for transfers between devices, per_device(): lax.all_to_all(slot_rows, 'seq', split_axis=0, concat_axis=0, tiled=True)  6.15 us
    dot_general x4, matrix products, per_device(): jnp.dot(feature_part, weight, preferred_element_type=jnp.float32)  4.95 us
  transfers between devices with their start and end apart: 9, of which 7 were waited for; matrix products, arithmetic and copies ran while one was open for 10% of the time, Pallas kernels for 0%

profile of v1, /device:TPU:0, one launch (start us, length us, event | category | flops | bytes accessed | tf_op | source)
XLA Modules:
  0.0 139.4 jit_solution(15358585351118157686)
XLA Ops:
  6.6 0.7 all-gather.2.cloned.1.call-update
  7.3 7.3 %all-to-all-start = ((bf16[8,32,512]{2,1,0:T(8,128)(2,1)}), bf16[8,32,512]{2,1,0:T(8,128)(2,1)S(1)}, u32[]{:S(2)}, u32[]{:S(2)}) async-start(bf16[8,32,512]{2,1,0:T(8,128)(2,1)} %bitcast.81), calls=%async_computation | async-start | bytes 524288 | tf_op jit(solution)/shard_map/all_to_all | solution.py:119
  14.6 0.7 compare_and_fusion.1
  15.3 1.0 sort.17
  16.3 0.8 reduce-window.18
  17.4 6.2 %all-to-all-done = bf16[8,32,512]{2,1,0:T(8,128)(2,1)S(1)} async-done(((bf16[8,32,512]{2,1,0:T(8,128)(2,1)}), bf16[8,32,512]{2,1,0:T(8,128)(2,1)S(1)}, u32[]{:S(2)}, u32[]{:S(2)}) %all-to-all-start) | async-done | bytes 262176 | tf_op jit(solution)/shard_map/all_to_all | solution.py:119
  23.5 0.6 gather_fusion
  24.1 0.1 bitcast_select_fusion
  24.3 0.6 fusion.53
  25.5 0.7 broadcast_compare_fusion
  26.2 0.6 slice.199
  26.8 0.1 maximum_select_fusion.1
  26.9 1.6 %collective-permute-start.1 = (bf16[256,1024]{1,0:T(8,128)(2,1)S(1)}, bf16[256,1024]{1,0:T(8,128)(2,1)S(1)}, u32[]{:S(2)}, u32[]{:S(2)}) collective-permute-start(bf16[256,1024]{1,0:T(8,128)(2,1)S(1)} %maximum_select_fusion.1), channel_id=1, source_target_pairs={{0,2},{1,3},{2,0},{3,1},{4,6},{5,7},{6,4},{7,5},{8,10},{9,11},{10,... | collective-permute-start | bytes 1572872 | tf_op jit(solution)/shard_map/ppermute | solution.py:13
  28.6 15.4 %collective-permute-done.1 = bf16[256,1024]{1,0:T(8,128)(2,1)S(1)} collective-permute-done((bf16[256,1024]{1,0:T(8,128)(2,1)S(1)}, bf16[256,1024]{1,0:T(8,128)(2,1)S(1)}, u32[]{:S(2)}, u32[]{:S(2)}) %collective-permute-start.1) | collective-permute-done | bytes 524320 | tf_op jit(solution)/shard_map/ppermute | solution.py:13
  44.0 0.4 fusion.41
  44.4 1.8 %reduce-window.19 = f32[6,2,128]{2,1,0:T(2,128)S(1)} reduce-window(f32[6,2,128]{2,1,0:T(2,128)S(1)} %reshape.288, f32[]{:T(128)} %constant.154.clone.1), window={size=1x1x128 pad=0_0x0_0x127_0}, to_apply=%region_3.4 | reduce-window | flops 195072 | bytes 12292 | tf_op jit(solution)/shard_map/reduce-window.1
  46.3 0.1 copy.40
  46.6 0.2 slice_reduce_fusion
  46.9 0.7 convolution_convert_fusion.2
  47.7 2.4 %convolution_convert_fusion = bf16[256,512]{1,0:T(8,128)(2,1)S(1)} fusion(bf16[2048,512]{1,0:T(8,128)(2,1)} %all-gather.2.cloned.1.call-done, bf16[256,1024]{1,0:T(8,128)(2,1)S(1)} %collective-permute-done.1, bf16[256,1024]{1,0:T(8,128)(2,1)S(1)} %maximum_select_fusion.1, pred[]{:T(512)S(6)} %eq.48), kind=kOutput, calls=%fused_computation.8 | convolution fusion | flops 541720576 | bytes 3407873 | tf_op jit(solution)/shard_map/dot_general | solution.py:132
  50.1 3.4 %collective-permute-start.2 = (bf16[3,896]{1,0:T(4,128)(2,1)S(1)}, bf16[3,896]{1,0:T(4,128)(2,1)S(1)}, u32[]{:S(2)}, u32[]{:S(2)}) collective-permute-start(bf16[3,896]{1,0:T(4,128)(2,1)S(1)} %pad_maximum_fusion.3), channel_id=1, source_target_pairs={{0,4},{4,8},{8,12},{12,16},{16,20},{20,24},{24,28},{1,5},{5,9},{9,... | collective-permute-start | bytes 16136 | tf_op jit(solution)/shard_map/ppermute | solution.py:24
  53.4 0.7 broadcast_select_fusion.1
  54.1 0.7 collective-permute-done.2
  54.9 0.7 divide_multiply_fusion
  55.6 0.2 copy.39
  55.8 0.5 fusion.25
  56.4 0.8 pad_maximum_fusion
  57.2 5.9 %collective-permute-start.4 = (f32[6,65,256]{2,1,0:T(8,128)}, f32[6,65,256]{2,1,0:T(8,128)}, u32[]{:S(2)}, u32[]{:S(2)}) collective-permute-start(f32[6,65,256]{2,1,0:T(8,128)} %pad_maximum_fusion), channel_id=1, source_target_pairs={{0,8},{4,12},{8,16},{12,20},{16,24},{20,28},{1,9},{5,13},{9,17},{1... | collective-permute-start | bytes 1198088 | tf_op jit(solution)/shard_map/ppermute | solution.py:24
  63.1 3.2 %collective-permute-start.3 = (f32[6,65,256]{2,1,0:T(8,128)}, f32[6,65,256]{2,1,0:T(8,128)}, u32[]{:S(2)}, u32[]{:S(2)}) collective-permute-start(f32[6,65,256]{2,1,0:T(8,128)} %pad_maximum_fusion), channel_id=1, source_target_pairs={{0,4},{4,8},{8,12},{12,16},{16,20},{20,24},{24,28},{1,5},{5,9},{9,... | collective-permute-start | bytes 1198088 | tf_op jit(solution)/shard_map/ppermute | solution.py:24
  66.4 0.8 fusion.49
  67.2 0.1 fusion.31
  67.3 3.7 %collective-permute-done.4 = f32[6,65,256]{2,1,0:T(8,128)} collective-permute-done((f32[6,65,256]{2,1,0:T(8,128)}, f32[6,65,256]{2,1,0:T(8,128)}, u32[]{:S(2)}, u32[]{:S(2)}) %collective-permute-start.4) | collective-permute-done | bytes 399392 | tf_op jit(solution)/shard_map/ppermute | solution.py:24
  71.0 3.0 %collective-permute-done.3 = f32[6,65,256]{2,1,0:T(8,128)} collective-permute-done((f32[6,65,256]{2,1,0:T(8,128)}, f32[6,65,256]{2,1,0:T(8,128)}, u32[]{:S(2)}, u32[]{:S(2)}) %collective-permute-start.3) | collective-permute-done | bytes 399392 | tf_op jit(solution)/shard_map/ppermute | solution.py:24
  73.9 0.8 fusion.47
  74.8 1.2 slice_add_fusion
  76.0 10.9 %collective-permute-start.5 = (f32[6,65,256]{2,1,0:T(8,128)S(1)}, f32[6,65,256]{2,1,0:T(8,128)S(1)}, u32[]{:S(2)}, u32[]{:S(2)}) collective-permute-start(f32[6,65,256]{2,1,0:T(8,128)S(1)} %pad_maximum_fusion.1), channel_id=1, source_target_pairs={{0,8},{4,12},{8,16},{12,20},{16,24},{20,28},{1,9},{5,13},{9,17},{1... | collective-permute-start | bytes 1198088 | tf_op jit(solution)/shard_map/ppermute | solution.py:24
  87.0 1.5 %fusion.10 = f32[256,384]{1,0:T(8,128)} fusion(bf16[2048,384]{1,0:T(8,128)(2,1)S(1)} %copy-done.6, bf16[256,1024]{1,0:T(8,128)(2,1)S(1)} %copy-done.8, bf16[256,1024]{1,0:T(8,128)(2,1)S(1)} %copy-done.2, pred[]{:T(512)S(6)} %eq.48), kind=kOutput, calls=%fused_computation.13 | convolution fusion | flops 407568384 | bytes 3014657 | tf_op jit(solution)/shard_map/dot_general | solution.py:132
  88.5 5.9 %collective-permute-done.5 = f32[6,65,256]{2,1,0:T(8,128)S(1)} collective-permute-done((f32[6,65,256]{2,1,0:T(8,128)S(1)}, f32[6,65,256]{2,1,0:T(8,128)S(1)}, u32[]{:S(2)}, u32[]{:S(2)}) %collective-permute-start.5) | collective-permute-done | bytes 399392 | tf_op jit(solution)/shard_map/ppermute | solution.py:24
  94.5 5.3 %collective-permute-start.6 = (f32[6,65,256]{2,1,0:T(8,128)S(1)}, f32[6,65,256]{2,1,0:T(8,128)S(1)}, u32[]{:S(2)}, u32[]{:S(2)}) collective-permute-start(f32[6,65,256]{2,1,0:T(8,128)S(1)} %pad_maximum_fusion.2), channel_id=1, source_target_pairs={{0,16},{4,20},{8,24},{12,28},{1,17},{5,21},{9,25},{13,29},{2,18},{... | collective-permute-start | bytes 1198088 | tf_op jit(solution)/shard_map/ppermute | solution.py:24
  99.8 0.4 fusion.33
  100.3 1.9 %fusion.5 = f32[256,6,64]{0,2,1:T(8,128)S(1)} fusion(f32[6,256]{1,0:T(8,128)S(1)} %bitcast.86, f32[256,256]{1,0:T(8,128)S(1)} %fusion.33, pred[256,256]{1,0:T(8,128)(4,1)S(1)} %fusion.31, f32[256,6,64]{0,2,1:T(8,128)S(1)} %bitcast.76, f32[256,6]{0,1:T(8,128)S(1)} %get-tuple-element.76), kind=kOutput, calls=%fused_computation.7 | convolution fusion | flops 303267840 | bytes 1126400 | tf_op jit(solution)/shard_map/hts,shp->thp/dot_general | solution.py:87
  102.1 4.3 %collective-permute-done.6 = f32[6,65,256]{2,1,0:T(8,128)S(1)} collective-permute-done((f32[6,65,256]{2,1,0:T(8,128)S(1)}, f32[6,65,256]{2,1,0:T(8,128)S(1)}, u32[]{:S(2)}, u32[]{:S(2)}) %collective-permute-start.6) | collective-permute-done | bytes 399392 | tf_op jit(solution)/shard_map/ppermute | solution.py:24
  106.4 0.5 fusion.9
  106.9 0.2 copy.42
  107.1 1.1 multiply_convert_fusion
  108.2 0.6 gather_fusion.1
  108.9 22.9 %all_to_all.10 = bf16[8,32,384]{2,1,0:T(8,128)(2,1)S(1)} all-to-all(bf16[8,32,384]{2,1,0:T(8,128)(2,1)S(1)} %broadcast_select_fusion), channel_id=1, replica_groups=mesh['seq'=8,'fsdp'=4] {'seq'}, dimensions={0} | all-to-all | bytes 393216 | tf_op jit(solution)/shard_map/all_to_all | solution.py:171
  131.9 0.7 copy.63
  (62 shorter events, 1.4 us)
Async XLA Ops:
  6.5 40.4 %copy-start = (bf16[2048,384]{1,0:T(8,128)(2,1)S(1)}, bf16[2048,384]{1,0:T(8,128)(2,1)}, u32[]{:S(2)}) copy-start(bf16[2048,384]{1,0:T(8,128)(2,1)} %param.23) | copy-start | bytes 4718596
  6.5 22.0 %copy-start.4 = (f32[4,384]{1,0:T(4,128)S(1)}, f32[4,384]{1,0:T(4,128)}, u32[]{:S(2)}) copy-start(f32[4,384]{1,0:T(4,128)} %param.27) | copy-start | bytes 18436
  6.5 22.0 %copy-start.3 = (f32[4,512]{1,0:T(4,128)S(1)}, f32[4,512]{1,0:T(4,128)}, u32[]{:S(2)}) copy-start(f32[4,512]{1,0:T(4,128)} %param.28) | copy-start | bytes 24580
  6.5 22.0 %copy-start.10 = (f32[6]{0:T(128)S(1)}, f32[6]{0:T(128)}, u32[]{:S(2)}) copy-start(f32[6]{0:T(128)} %param.30) | copy-start | bytes 76
  6.5 37.4 %copy-start.11 = (f32[6]{0:T(128)S(1)}, f32[6]{0:T(128)}, u32[]{:S(2)}) copy-start(f32[6]{0:T(128)} %param.29) | copy-start | bytes 76
  6.5 37.4 %copy-start.9 = (bf16[2048,6]{0,1:T(8,128)(2,1)S(1)}, bf16[2048,6]{0,1:T(8,128)(2,1)}, u32[]{:S(2)}) copy-start(bf16[2048,6]{0,1:T(8,128)(2,1)} %param.26) | copy-start | bytes 73732
  6.6 41.1 %all-gather.2.cloned.1.call-start = ((), (), s32[]{:S(2)}) async-start(), calls=%async_computation.2 | async-start | bytes 2621440 | tf_op jit(solution)/shard_map/all_gather | solution.py:127
  7.3 16.2 %all-to-all-start = ((bf16[8,32,512]{2,1,0:T(8,128)(2,1)}), bf16[8,32,512]{2,1,0:T(8,128)(2,1)S(1)}, u32[]{:S(2)}, u32[]{:S(2)}) async-start(bf16[8,32,512]{2,1,0:T(8,128)(2,1)} %bitcast.81), calls=%async_computation | async-start | bytes 524288 | tf_op jit(solution)/shard_map/all_to_all | solution.py:119
  24.2 2.6 %collective-permute-start = (bf16[256,512]{1,0:T(8,128)(2,1)S(1)}, bf16[256,512]{1,0:T(8,128)(2,1)S(1)}, u32[]{:S(2)}, u32[]{:S(2)}) collective-permute-start(bf16[256,512]{1,0:T(8,128)(2,1)S(1)} %bitcast_select_fusion), channel_id=1, source_target_pairs={{0,1},{1,0},{2,3},{3,2},{4,5},{5,4},{6,7},{7,6},{8,9},{9,8},{10,11... | collective-permute-start | bytes 786440 | tf_op jit(solution)/shard_map/ppermute | solution.py:13
  26.9 20.7 %copy-start.1 = (bf16[256,1024]{1,0:T(8,128)(2,1)}, bf16[256,1024]{1,0:T(8,128)(2,1)S(1)}, u32[]{:S(2)}) copy-start(bf16[256,1024]{1,0:T(8,128)(2,1)S(1)} %maximum_select_fusion.1) | copy-start | bytes 1572868
  26.9 17.0 %collective-permute-start.1 = (bf16[256,1024]{1,0:T(8,128)(2,1)S(1)}, bf16[256,1024]{1,0:T(8,128)(2,1)S(1)}, u32[]{:S(2)}, u32[]{:S(2)}) collective-permute-start(bf16[256,1024]{1,0:T(8,128)(2,1)S(1)} %maximum_select_fusion.1), channel_id=1, source_target_pairs={{0,2},{1,3},{2,0},{3,1},{4,6},{5,7},{6,4},{7,5},{8,10},{9,11},{10,... | collective-permute-start | bytes 1572872 | tf_op jit(solution)/shard_map/ppermute | solution.py:13
  44.0 3.7 %copy-start.7 = (bf16[256,1024]{1,0:T(8,128)(2,1)}, bf16[256,1024]{1,0:T(8,128)(2,1)S(1)}, u32[]{:S(2)}) copy-start(bf16[256,1024]{1,0:T(8,128)(2,1)S(1)} %collective-permute-done.1) | copy-start | bytes 1572868
  50.1 4.7 %collective-permute-start.2 = (bf16[3,896]{1,0:T(4,128)(2,1)S(1)}, bf16[3,896]{1,0:T(4,128)(2,1)S(1)}, u32[]{:S(2)}, u32[]{:S(2)}) collective-permute-start(bf16[3,896]{1,0:T(4,128)(2,1)S(1)} %pad_maximum_fusion.3), channel_id=1, source_target_pairs={{0,4},{4,8},{8,12},{12,16},{16,20},{20,24},{24,28},{1,5},{5,9},{9,... | collective-permute-start | bytes 16136 | tf_op jit(solution)/shard_map/ppermute | solution.py:24
  55.8 31.2 %copy-start.2 = (bf16[256,1024]{1,0:T(8,128)(2,1)S(1)}, bf16[256,1024]{1,0:T(8,128)(2,1)}, u32[]{:S(2)}) copy-start(bf16[256,1024]{1,0:T(8,128)(2,1)} %copy-done.1) | copy-start | bytes 1572868
  57.2 13.8 %collective-permute-start.4 = (f32[6,65,256]{2,1,0:T(8,128)}, f32[6,65,256]{2,1,0:T(8,128)}, u32[]{:S(2)}, u32[]{:S(2)}) collective-permute-start(f32[6,65,256]{2,1,0:T(8,128)} %pad_maximum_fusion), channel_id=1, source_target_pairs={{0,8},{4,12},{8,16},{12,20},{16,24},{20,28},{1,9},{5,13},{9,17},{1... | collective-permute-start | bytes 1198088 | tf_op jit(solution)/shard_map/ppermute | solution.py:24
  63.1 10.9 %collective-permute-start.3 = (f32[6,65,256]{2,1,0:T(8,128)}, f32[6,65,256]{2,1,0:T(8,128)}, u32[]{:S(2)}, u32[]{:S(2)}) collective-permute-start(f32[6,65,256]{2,1,0:T(8,128)} %pad_maximum_fusion), channel_id=1, source_target_pairs={{0,4},{4,8},{8,12},{12,16},{16,20},{20,24},{24,28},{1,5},{5,9},{9,... | collective-permute-start | bytes 1198088 | tf_op jit(solution)/shard_map/ppermute | solution.py:24
  66.4 20.6 %copy-start.6 = (bf16[2048,384]{1,0:T(8,128)(2,1)S(1)}, bf16[2048,384]{1,0:T(8,128)(2,1)}, u32[]{:S(2)}) copy-start(bf16[2048,384]{1,0:T(8,128)(2,1)} %param.24) | copy-start | bytes 4718596
  66.4 20.6 %copy-start.8 = (bf16[256,1024]{1,0:T(8,128)(2,1)S(1)}, bf16[256,1024]{1,0:T(8,128)(2,1)}, u32[]{:S(2)}) copy-start(bf16[256,1024]{1,0:T(8,128)(2,1)} %copy-done.7) | copy-start | bytes 1572868
  76.0 18.4 %collective-permute-start.5 = (f32[6,65,256]{2,1,0:T(8,128)S(1)}, f32[6,65,256]{2,1,0:T(8,128)S(1)}, u32[]{:S(2)}, u32[]{:S(2)}) collective-permute-start(f32[6,65,256]{2,1,0:T(8,128)S(1)} %pad_maximum_fusion.1), channel_id=1, source_target_pairs={{0,8},{4,12},{8,16},{12,20},{16,24},{20,28},{1,9},{5,13},{9,17},{1... | collective-permute-start | bytes 1198088 | tf_op jit(solution)/shard_map/ppermute | solution.py:24
  94.5 11.9 %copy-start.5 = (f32[6]{0:T(128)S(1)}, f32[6]{0:T(128)}, u32[]{:S(2)}) copy-start(f32[6]{0:T(128)} %param.31) | copy-start | bytes 76
  94.5 11.9 %collective-permute-start.6 = (f32[6,65,256]{2,1,0:T(8,128)S(1)}, f32[6,65,256]{2,1,0:T(8,128)S(1)}, u32[]{:S(2)}, u32[]{:S(2)}) collective-permute-start(f32[6,65,256]{2,1,0:T(8,128)S(1)} %pad_maximum_fusion.2), channel_id=1, source_target_pairs={{0,16},{4,20},{8,24},{12,28},{1,17},{5,21},{9,25},{13,29},{2,18},{... | collective-permute-start | bytes 1198088 | tf_op jit(solution)/shard_map/ppermute | solution.py:24
Sparse Core Ops, SparseCore 0:
  9.0 28.0 all-gather.1
